TPU v7x, 32 devices: a whole 2x2x4 slice. The times are simulated.
32 devices in a mesh: groups: 2 (over y), gx: 4 (over z), gz: 2 (over x), vert: 2 (over core).
Axes of the slice: x: 2, y: 2, z: 4, core: 2. Of those that a mesh axis runs over, the one named last changes fastest.
Arguments:
- flow_field: bfloat16 [4, 4, 5, 4, 256, 256], P('groups', 'vert', None, 'gx', None, 'gz'), parts along dimension 0, may hold values from -6 to 6
- test_streams: int32 [4], P('groups'), parts along dimension 0, may hold values from 0 to 999999
- snapshot_ids: int32 [4, 4], P('groups', 'vert'), parts along dimension 0, may hold values from 0 to 65535
Outputs:
- sketch_x: float32 [8, 128], P(('groups', 'gx')), parts along dimension 0
- sketch_y: float32 [512, 128], P(('groups', 'gx', 'gz', 'vert')), parts along dimension 0
- sketch_z: float32 [512, 128], P(('groups', 'gz'), ('gx', 'vert')), parts along dimension 0
- core_sketch: float32 [4608, 2, 48], P(('groups', 'gx')), parts along dimension 0
There are 2 independent parts, one for each index of `groups`. A program takes and returns all parts, laid end to end along the dimension named above; each array names one. Nothing has to cross between parts.
All inputs are finite; a program needn't handle non-finite values.
Results may differ from a plain program's by a relative error of at most 0.007.
Values sent between devices are 32-bit elements; how exact they have to be, the bound alone decides.
No kernel may reach another device: no remote copies, remote signals or barrier semaphores. Data moves between devices by JAX's collectives and lax.ppermute only.
A program may use at most 64 MiB of HBM per device.

v0:
```python
import math
import jax
import jax.numpy as jnp
from jax import lax
from jax.sharding import PartitionSpec as P

K = 128
S = 48
E = 2


def hash_index(index, stream, salt):
    mixed = index * -1640531535 + stream * -2048144777 + salt
    mixed = jnp.bitwise_xor(mixed, lax.shift_right_logical(mixed, jnp.int32(16)))
    mixed = mixed * 739982445
    mixed = jnp.bitwise_xor(mixed, lax.shift_right_logical(mixed, jnp.int32(13)))
    mixed = mixed * 695872825
    return jnp.bitwise_xor(mixed, lax.shift_right_logical(mixed, jnp.int32(16)))


def unit_value(index, stream, salt):
    upper = lax.shift_right_logical(hash_index(index, stream, salt), jnp.int32(9))
    return ((2 * upper + 1).astype(jnp.float32) * 2.0 ** (-24) - 1.0).astype(jnp.bfloat16)


def test_table(row_ids, col_ids, stride, stream, salt):
    return unit_value(row_ids[:, None] * stride + col_ids[None, :], stream, salt)


def shards(flow_field, test_streams, snapshot_ids):
    highest = lax.Precision.HIGHEST
    batches, local_snaps, variables, cells_x, cells_y, cells_z = flow_field.shape
    slabs_x = lax.axis_size("gx")
    total_x = cells_x * slabs_x
    total_z = cells_z * lax.axis_size("gz")
    total_q = variables * batches * local_snaps * lax.axis_size("vert")
    factor_stream = test_streams[0]
    core_stream = test_streams[1]
    rank_ids = jnp.arange(K, dtype=jnp.int32)
    sketch_ids = jnp.arange(S, dtype=jnp.int32)
    x_ids = lax.axis_index("gx") * cells_x + jnp.arange(cells_x, dtype=jnp.int32)
    y_ids = jnp.arange(cells_y, dtype=jnp.int32)
    z_ids = lax.axis_index("gz") * cells_z + jnp.arange(cells_z, dtype=jnp.int32)
    ax_tab = test_table(x_ids, rank_ids, K, factor_stream, 1).astype(jnp.float32)
    ay_low = test_table(y_ids, rank_ids, K, factor_stream, 2)
    az_low = test_table(z_ids, rank_ids, K, factor_stream, 3)
    ay_tab = ay_low.astype(jnp.float32)
    phy_low = test_table(sketch_ids, y_ids, cells_y, core_stream, 6)
    phz_low = test_table(sketch_ids, z_ids, total_z, core_stream, 7)

    def batch_terms(batch_idx):
        blocks = flow_field[batch_idx].reshape(-1, cells_x, cells_y, cells_z)
        pairs = blocks.shape[0]
        q_ids = (
            snapshot_ids[batch_idx][:, None] * variables
            + jnp.arange(variables, dtype=jnp.int32)[None, :]
        ).reshape(-1)
        aq_tab = test_table(q_ids, rank_ids, K, factor_stream, 4).astype(jnp.float32)
        phq_low = test_table(q_ids, jnp.arange(E, dtype=jnp.int32), E, core_stream, 8)
        rows_z = blocks.reshape(-1, cells_z)
        along_z = jnp.dot(rows_z, az_low, preferred_element_type=jnp.float32).reshape(
            pairs, cells_x, cells_y, K
        )
        along_y = jnp.einsum("qxyz,yk->qxzk", blocks, ay_low, preferred_element_type=jnp.float32)
        weights = aq_tab[:, None, :] * ax_tab[None, :, :]
        part_x = jnp.sum(
            jnp.sum(along_z * ay_tab[None, None, :, :], axis=2) * aq_tab[:, None, :], axis=0
        )
        part_y = jnp.sum(along_z * weights[:, :, None, :], axis=(0, 1))
        part_z = jnp.sum(along_y * weights[:, :, None, :], axis=(0, 1))
        first = jnp.dot(rows_z, phz_low.T, preferred_element_type=jnp.float32).reshape(
            pairs, cells_x, cells_y, S
        )
        second = jnp.einsum("qxyc,by->qxbc", first, phy_low.astype(jnp.float32), precision=highest)
        partial_core = jnp.einsum(
            "qxbc,qe->bcex", second, phq_low.astype(jnp.float32), precision=highest
        )
        return (part_x, part_y, part_z, partial_core.reshape(S * S, E, cells_x))

    def finish(part_x, part_y, part_z, partial_core):
        summed, sum_x = lax.psum((partial_core, part_x), ("gz", "vert"))
        phx_whole = test_table(
            sketch_ids, jnp.arange(total_x, dtype=jnp.int32), total_x, core_stream, 5
        ).astype(jnp.float32)
        core = jnp.einsum(
            "rex,ax->rea",
            lax.all_to_all(summed, "gx", split_axis=0, concat_axis=2, tiled=True),
            phx_whole,
            precision=highest,
        )
        sum_z = lax.psum_scatter(part_z, ("gx", "vert"), scatter_dimension=1, tiled=True)
        sum_y = lax.psum_scatter(part_y, ("gx", "gz", "vert"), scatter_dimension=0, tiled=True)
        return (sum_x, sum_y, sum_z, core)

    terms = [batch_terms(batch_idx) for batch_idx in range(batches)]
    totals = finish(terms[0][0], terms[0][1], terms[0][2], terms[0][3])
    for later in terms[1:]:
        latest = finish(later[0], later[1], later[2], later[3])
        totals = tuple((earlier + newer for earlier, newer in zip(totals, latest)))
    scale_x = 3.0**1.5 / math.sqrt(cells_y * total_z * total_q)
    scale_y = 3.0**1.5 / math.sqrt(total_x * total_z * total_q)
    scale_z = 3.0**1.5 / math.sqrt(total_x * cells_y * total_q)
    scale_core = 9.0 / math.sqrt(total_x * cells_y * total_z * total_q)
    return (totals[0] * scale_x, totals[1] * scale_y, totals[2] * scale_z, totals[3] * scale_core)


def solution(mesh):
    in_specs = (P("groups", "vert", None, "gx", None, "gz"), P("groups"), P("groups", "vert"))
    out_specs = (
        P(("groups", "gx"), None),
        P(("groups", "gx", "gz", "vert"), None),
        P(("groups", "gz"), ("gx", "vert")),
        P(("groups", "gx"), None, None),
    )
    return jax.shard_map(shards, mesh=mesh, in_specs=in_specs, out_specs=out_specs, check_vma=False)
```

profile of v0, /device:TPU:0, one launch (start us, length us, event | category | flops | bytes accessed | tf_op | source)
XLA Modules:
  0.0 124.9 jit_solution(1838660358389235373)
XLA Ops:
  7.2 1.3 %fusion.295 = (s32[1]{0:T(128)}, s32[1]{0:T(128)}) fusion(s32[2]{0:T(128)} %param.4), kind=kLoop, calls=%fused_computation.343 | loop fusion | bytes 16 | tf_op jit(solution)/shard_map/slice | solution.py:38
  8.5 0.8 multiply_bitcast_fusion
  9.4 0.1 mul.691
  9.5 0.1 mul.680
  9.6 1.4 %fusion.294 = (bf16[1,2,5,1,256,128]{5,4,3,2,1,0:T(8,128)(2,1)S(1)}, bf16[1,2,5,1,256,128]{5,4,3,2,1,0:T(8,128)(2,1)S(1)}) fusion(bf16[2,2,5,1,256,128]{5,4,3,2,1,0:T(8,128)(2,1)} %param.3), kind=kLoop, calls=%fused_computation.342 | loop fusion | bytes 2621440 | tf_op jit(solution)/shard_map/slice | solution.py:52
  11.7 0.1 convert_multiply_fusion
  11.8 0.3 fusion.2
  12.1 0.3 fusion.3
  12.4 0.6 add.598
  13.8 1.2 fusion.68
  15.0 0.4 fusion.66
  15.4 0.5 convolution_bitcast_fusion
  15.8 1.5 %convolution_bitcast_fusion.1 = f32[2560,128]{0,1:T(8,128)} fusion(bf16[2560,128]{1,0:T(8,128)(2,1)S(1)} %bitcast.111, s32[]{:T(128)} %bitcast, s32[128]{0:T(128)S(1)} %broadcast_multiply_fusion.3), kind=kOutput, calls=%fused_computation.1 | convolution fusion | flops 84197376 | bytes 1966596 | tf_op jit(solution)/shard_map/dot_general | solution.py:61
  17.5 0.1 copy.23
  17.6 0.6 convolution_bitcast_fusion.5
  18.3 0.3 convolution_bitcast_fusion.7
  18.6 0.1 reshape.486
  18.7 0.6 convolution_bitcast_fusion.4
  19.3 0.3 convolution_bitcast_fusion.6
  19.6 0.1 reshape.489
  19.8 1.5 %copy.24 = f32[2560,128]{1,0:T(8,128)} copy(f32[2560,128]{0,1:T(8,128)S(1)} %convolution_bitcast_fusion) | data formatting | bytes 2621440 | tf_op jit(solution)/shard_map/dot_general | solution.py:61
  21.2 1.5 %copy.22 = f32[2560,128]{1,0:T(8,128)} copy(f32[2560,128]{0,1:T(8,128)S(1)} %copy-done) | data formatting | bytes 2621440 | tf_op jit(solution)/shard_map/dot_general | solution.py:61
  22.7 1.7 %multiply_reduce_fusion = (f32[256,128]{1,0:T(8,128)S(1)}, f32[10,128]{1,0:T(8,128)S(1)}, f32[10,128]{1,0:T(8,128)S(1)}, f32[256,128]{1,0:T(8,128)S(1)}) fusion(f32[10,1,256,128]{3,2,0,1:T(8,128)S(1)} %bitcast.115, f32[10,128]{1,0:T(8,128)S(1)} %get-tuple-element.23, f32[256,128]{1,0:T(8,128)S(1)} %copy.23, f32[10,1,256,128]{3,2,0,1:T(8,128)} %bitcast.116, ...), kind=kLoop, calls=%fused_computation.2 | loop fusion | flops 2553344 | bytes 3035136 | tf_op jit(solution)/shard_map/reduce_sum | solution.py:69
  24.4 0.1 fusion.70
  24.6 13.2 %all-reduce = (f32[1,128]{1,0:T(1,128)S(1)}, f32[2304,2,1]{0,1,2:T(2,128)S(1)}, f32[2304,2,1]{0,1,2:T(2,128)S(1)}) all-reduce(f32[1,128]{1,0:T(1,128)S(1)} %add_bitcast_fusion, f32[2304,2,1]{0,1,2:T(2,128)S(1)} %reshape.486, f32[2304,2,1]{0,1,2:T(2,128)S(1)} %reshape.489), channel_id=1, replica_groups=mesh['groups'=2,'gx'=4,'gz'=2,'vert'=2] {'gz','vert'}, use_global_device_ids=true, to_apply=%region_2.0 | all-reduce | flops 9344 | bytes 74752 | tf_op jit(solution)/shard_map/psum | solution.py:81
  37.7 1.5 %copy.28 = f32[2304,2,1]{1,2,0:T(1,128)S(1)} copy(f32[2304,2,1]{0,1,2:T(2,128)S(1)} %get-tuple-element.9) | data formatting | bytes 36864 | tf_op jit(solution)/shard_map/psum | solution.py:81
  39.2 0.5 broadcast.1041
  39.8 10.4 %reduce.10 = f32[2304,2]{1,0:T(8,128)S(1)} reduce(f32[2304,1,2]{2,1,0:T(1,128)S(1)} %bitcast.117, f32[]{:T(128)} %broadcast.1041), dimensions={1}, to_apply=%bitcast.99.reduce_sub_computation | reduce | bytes 36868
  50.2 1.3 %reshape.496 = f32[4,1,1152]{2,1,0:T(1,128)} reshape(f32[2304,2]{1,0:T(8,128)S(1)} %reduce.10) | data formatting | bytes 36864
  51.5 4.9 %all-to-all-start = ((f32[4,1,1152]{2,1,0:T(1,128)}), f32[4,1,1152]{2,1,0:T(1,128)S(1)}, u32[]{:S(2)}, u32[]{:S(2)}) async-start(f32[4,1,1152]{2,1,0:T(1,128)} %reshape.496), calls=%async_computation | async-start | bytes 36864 | tf_op jit(solution)/shard_map/all_to_all | solution.py:87
  56.4 0.7 add.597
  57.1 0.5 broadcast_multiply_fusion.2
  57.6 1.4 %copy.33 = f32[2304,2,1]{1,2,0:T(1,128)S(1)} copy(f32[2304,2,1]{0,1,2:T(2,128)S(1)} %get-tuple-element.10) | data formatting | bytes 36864 | tf_op jit(solution)/shard_map/psum | solution.py:81
  59.1 10.4 %reduce.12 = f32[2304,2]{1,0:T(8,128)S(1)} reduce(f32[2304,1,2]{2,1,0:T(1,128)S(1)} %bitcast.118, f32[]{:T(128)} %broadcast.1041), dimensions={1}, to_apply=%bitcast.101.reduce_sub_computation | reduce | bytes 36868
  69.5 1.3 %reshape.498 = f32[4,1,1152]{2,1,0:T(1,128)} reshape(f32[2304,2]{1,0:T(8,128)S(1)} %reduce.12) | data formatting | bytes 36864
  70.8 5.1 %all-to-all-start.1 = ((f32[4,1,1152]{2,1,0:T(1,128)}), f32[4,1,1152]{2,1,0:T(1,128)S(1)}, u32[]{:S(2)}, u32[]{:S(2)}) async-start(f32[4,1,1152]{2,1,0:T(1,128)} %reshape.498), calls=%async_computation.1 | async-start | bytes 36864 | tf_op jit(solution)/shard_map/all_to_all | solution.py:87
  75.9 0.7 reduce.11
  76.6 1.8 %reshape.497 = f32[2304,1,2]{2,1,0:T(1,128)S(1)} reshape(f32[4,1152]{1,0:T(4,128)S(1)} %reduce.11) | data formatting | bytes 36864
  78.5 0.4 copy.35
  78.9 2.7 %all-to-all-done.1 = f32[4,1,1152]{2,1,0:T(1,128)S(1)} async-done(((f32[4,1,1152]{2,1,0:T(1,128)}), f32[4,1,1152]{2,1,0:T(1,128)S(1)}, u32[]{:S(2)}, u32[]{:S(2)}) %all-to-all-start.1) | async-done | bytes 18464 | tf_op jit(solution)/shard_map/all_to_all | solution.py:87
  81.5 0.7 reduce.13
  82.2 1.8 %reshape.499 = f32[2304,1,2]{2,1,0:T(1,128)S(1)} reshape(f32[4,1152]{1,0:T(4,128)S(1)} %reduce.13) | data formatting | bytes 36864
  84.1 0.4 copy.36
  84.5 0.3 fusion.64
  84.8 1.0 fusion.4
  85.8 1.3 %broadcast_multiply_fusion = f32[128,16]{0,1:T(8,128)} fusion(f32[128,16]{0,1:T(8,128)} %reduce-scatter.5.cloned.1.call-done), kind=kLoop, calls=%fused_computation.117 | loop fusion | flops 2048 | bytes 16384 | tf_op jit(solution)/shard_map/mul | solution.py:104
  87.1 29.7 %reduce-scatter.3.cloned.1.call-done = f32[16,128]{1,0:T(8,128)} async-done(((f32[256,128]{1,0:T(8,128)}), f32[16,128]{1,0:T(8,128)}) %reduce-scatter.3.cloned.1.call-update) | async-done | bytes 8208 | tf_op jit(solution)/shard_map/reduce_scatter | solution.py:92
  116.8 1.3 %broadcast_multiply_fusion.1 = f32[16,128]{1,0:T(8,128)} fusion(f32[16,128]{1,0:T(8,128)} %reduce-scatter.3.cloned.1.call-done), kind=kLoop, calls=%fused_computation.118 | loop fusion | flops 2048 | bytes 16384 | tf_op jit(solution)/shard_map/mul | solution.py:104
  (26 shorter events, 0.6 us)
Async XLA Ops:
  7.2 78.7 %reduce-scatter.5.cloned.1.call-start = ((), (), s32[]{:S(2)}) async-start(), calls=%async_computation.5 | async-start | bytes 73728 | tf_op jit(solution)/shard_map/reduce_scatter | solution.py:91
  15.8 1.8 %copy-start.2 = (f32[48,2560]{1,0:T(8,128)S(1)}, f32[48,2560]{1,0:T(8,128)}, u32[]{:S(2)}) copy-start(f32[48,2560]{1,0:T(8,128)} %fusion.68) | copy-start | bytes 1474564
  19.7 1.5 %copy-start = (f32[2560,128]{0,1:T(8,128)S(1)}, f32[2560,128]{0,1:T(8,128)}, u32[]{:S(2)}) copy-start(f32[2560,128]{0,1:T(8,128)} %convolution_bitcast_fusion.1) | copy-start | bytes 3932164
  21.2 1.5 %copy-start.1 = (f32[2560,128]{1,0:T(8,128)S(1)}, f32[2560,128]{1,0:T(8,128)}, u32[]{:S(2)}) copy-start(f32[2560,128]{1,0:T(8,128)} %copy.24) | copy-start | bytes 3932164
  51.5 19.3 %all-to-all-start = ((f32[4,1,1152]{2,1,0:T(1,128)}), f32[4,1,1152]{2,1,0:T(1,128)S(1)}, u32[]{:S(2)}, u32[]{:S(2)}) async-start(f32[4,1,1152]{2,1,0:T(1,128)} %reshape.496), calls=%async_computation | async-start | bytes 36864 | tf_op jit(solution)/shard_map/all_to_all | solution.py:87
  56.4 60.4 %reduce-scatter.3.cloned.1.call-start = ((), (), s32[]{:S(2)}) async-start(), calls=%async_computation.4 | async-start | bytes 139264 | tf_op jit(solution)/shard_map/reduce_scatter | solution.py:92
  70.8 10.7 %all-to-all-start.1 = ((f32[4,1,1152]{2,1,0:T(1,128)}), f32[4,1,1152]{2,1,0:T(1,128)S(1)}, u32[]{:S(2)}, u32[]{:S(2)}) async-start(f32[4,1,1152]{2,1,0:T(1,128)} %reshape.498), calls=%async_computation.1 | async-start | bytes 36864 | tf_op jit(solution)/shard_map/all_to_all | solution.py:87
Sparse Core Ops, SparseCore 0:
  13.2 32.7 reduce-scatter.4
  61.1 55.6 reduce-scatter.2
where the time goes:
time: 125 us
  waiting for transfers between devices  32.4 us (26%)
  other arithmetic  29.6 us (24%)
  local copies, waits for them, and re-layouts  16.8 us (13%)
  between operations  15.6 us (12%)
  blocking collectives  13.2 us (11%)
  starting transfers between devices  10 us (8%)
  matrix products  7.37 us (6%)
    reduce_scatter x1, waiting for transfers between devices, finish(): lax.psum_scatter(part_y, ('gx', 'gz', 'vert'), scatter_dimension=0, tiled...  29.7 us
    unnamed x2, other arithmetic  20.9 us
    psum x1, blocking collectives, finish(): summed, sum_x = lax.psum((partial_core, part_x), ('gz', 'vert'))  13.2 us
    all_to_all x2, starting transfers between devices, finish(): lax.all_to_all(summed, 'gx', split_axis=0, concat_axis=2, tiled=True)  9.97 us
    unnamed x11, local copies, waits for them, and re-layouts  6.86 us
    dot_general x2, local copies, waits for them, and re-layouts, batch_terms(): jnp.dot(rows_z, az_low, preferred_element_type=jnp.float32)  2.95 us
    psum x2, local copies, waits for them, and re-layouts, finish(): summed, sum_x = lax.psum((partial_core, part_x), ('gz', 'vert'))  2.89 us
    all_to_all x2, waiting for transfers between devices, finish(): lax.all_to_all(summed, 'gx', split_axis=0, concat_axis=2, tiled=True)  2.68 us
  transfers between devices with their start and end apart: 4, of which 2 were waited for; matrix products, arithmetic and copies ran while one was open for 38% of the time, Pallas kernels for 0%

commit v1 on v0

--- a/solution.py
+++ b/solution.py
@@ -84,7 +84,12 @@
         ).astype(jnp.float32)
         core = jnp.einsum(
             "rex,ax->rea",
-            lax.all_to_all(summed, "gx", split_axis=0, concat_axis=2, tiled=True),
+            jnp.concatenate(
+                lax.all_to_all(
+                    jnp.stack(jnp.split(summed, lax.axis_size("gx"), axis=0)), "gx", 0, 0
+                ),
+                axis=2,
+            ),
             phx_whole,
             precision=highest,
         )

time: 125 us -> 112 us (0.90)
  other arithmetic: 29.6 us -> 8.57 us
  waiting for transfers between devices: 32.4 us -> 52.6 us
  local copies, waits for them, and re-layouts: 16.8 us -> 6.42 us
  starting transfers between devices: 10 us -> 8.22 us
    unnamed x2 -> x0, other arithmetic: 20.9 us -> none
    reduce_scatter x1, waiting for transfers between devices: 29.7 us -> 43.6 us  [finish(): lax.psum_scatter(part_y, ('gx', 'gz', 'vert'), scatter_dimension=0, tiled...]
    unnamed x11 -> x6, local copies, waits for them, and re-layouts: 6.86 us -> 0.01 us
    all_to_all x2, waiting for transfers between devices: 2.68 us -> 8.94 us  [finish(): lax.all_to_all(jnp.stack(jnp.split(summed, lax.axis_size('gx'), axis=0)),...]
    psum x2 -> x0, local copies, waits for them, and re-layouts: 2.89 us -> none  [finish(): summed, sum_x = lax.psum((partial_core, part_x), ('gz', 'vert'))]
    all_to_all x2, starting transfers between devices: 9.97 us -> 8.19 us  [finish(): lax.all_to_all(jnp.stack(jnp.split(summed, lax.axis_size('gx'), axis=0)),...]
    all_to_all x2 -> x0, other arithmetic: 1.4 us -> none  [finish(): lax.all_to_all(summed, 'gx', split_axis=0, concat_axis=2, tiled=True)]
  transfers between devices with their start and end apart: 4 -> 4, of which waited for: 2 -> 3; matrix products, arithmetic and copies ran while one was open for 38% -> 14% of each run, Pallas kernels for 0% -> 0%
where the time goes in v1:
time: 112 us
  waiting for transfers between devices  52.6 us (47%)
  between operations  15.5 us (14%)
  blocking collectives  13.2 us (12%)
  other arithmetic  8.57 us (8%)
  starting transfers between devices  8.22 us (7%)
  matrix products  7.36 us (7%)
  local copies, waits for them, and re-layouts  6.42 us (6%)
    reduce_scatter x1, waiting for transfers between devices, finish(): lax.psum_scatter(part_y, ('gx', 'gz', 'vert'), scatter_dimension=0, tiled...  43.6 us
    psum x1, blocking collectives, finish(): summed, sum_x = lax.psum((partial_core, part_x), ('gz', 'vert'))  13.2 us
    all_to_all x2, waiting for transfers between devices, finish(): lax.all_to_all(jnp.stack(jnp.split(summed, lax.axis_size('gx'), axis=0)),...  8.94 us
    all_to_all x2, starting transfers between devices, finish(): lax.all_to_all(jnp.stack(jnp.split(summed, lax.axis_size('gx'), axis=0)),...  8.19 us
    dot_general x2, local copies, waits for them, and re-layouts, batch_terms(): jnp.dot(rows_z, az_low, preferred_element_type=jnp.float32)  2.95 us
  transfers between devices with their start and end apart: 4, of which 3 were waited for; matrix products, arithmetic and copies ran while one was open for 14% of the time, Pallas kernels for 0%

profile of v1, /device:TPU:0, one launch (start us, length us, event | category | flops | bytes accessed | tf_op | source)
XLA Modules:
  0.0 111.8 jit_solution(16672092749914957688)
XLA Ops:
  7.2 0.0 reduce-scatter.5.cloned.1.call-start
  7.2 1.3 %fusion.297 = (s32[1]{0:T(128)}, s32[1]{0:T(128)}) fusion(s32[2]{0:T(128)} %param.4), kind=kLoop, calls=%fused_computation.355 | loop fusion | bytes 16 | tf_op jit(solution)/shard_map/slice | solution.py:38
  8.5 0.8 multiply_bitcast_fusion
  9.3 0.1 fusion.120
  9.4 0.1 mul.691
  9.5 0.1 fusion.122
  9.5 0.1 mul.680
  9.6 1.4 %fusion.296 = (bf16[1,2,5,1,256,128]{5,4,3,2,1,0:T(8,128)(2,1)S(1)}, bf16[1,2,5,1,256,128]{5,4,3,2,1,0:T(8,128)(2,1)S(1)}) fusion(bf16[2,2,5,1,256,128]{5,4,3,2,1,0:T(8,128)(2,1)} %param.3), kind=kLoop, calls=%fused_computation.354 | loop fusion | bytes 2621440 | tf_op jit(solution)/shard_map/slice | solution.py:52
  11.7 0.1 convert_multiply_fusion
  11.8 0.3 fusion.2
  12.1 0.3 fusion.3
  12.4 0.6 add.598
  13.0 0.0 reduce-scatter.5.cloned.1.call-update
  13.1 0.1 fusion.32
  13.8 1.2 %fusion.70 = f32[48,2560]{1,0:T(8,128)} fusion(bf16[2560,128]{1,0:T(8,128)(2,1)S(1)} %bitcast.120, s32[]{:T(128)} %bitcast.15, s32[128]{0:T(128)S(1)} %iota_add_fusion.2, s32[48]{0:T(128)S(1)} %iota_multiply_fusion.2), kind=kOutput, calls=%fused_computation.90 | convolution fusion | flops 31574016 | bytes 1147588 | tf_op jit(solution)/shard_map/dot_general | solution.py:71
  15.0 0.4 fusion.68
  15.4 0.5 convolution_bitcast_fusion
  15.8 1.5 %convolution_bitcast_fusion.1 = f32[2560,128]{0,1:T(8,128)} fusion(bf16[2560,128]{1,0:T(8,128)(2,1)S(1)} %bitcast.121, s32[]{:T(128)} %bitcast, s32[128]{0:T(128)S(1)} %broadcast_multiply_fusion.3), kind=kOutput, calls=%fused_computation.1 | convolution fusion | flops 84197376 | bytes 1966596 | tf_op jit(solution)/shard_map/dot_general | solution.py:61
  17.4 0.1 mul.763
  17.5 0.1 mul.727
  17.5 0.1 copy.37
  17.6 0.6 convolution_bitcast_fusion.5
  18.3 0.3 convolution_bitcast_fusion.7
  18.6 0.1 reshape.498
  18.7 0.6 convolution_bitcast_fusion.4
  19.3 0.3 convolution_bitcast_fusion.6
  19.6 0.1 reshape.503
  19.8 1.5 %copy.38 = f32[2560,128]{1,0:T(8,128)} copy(f32[2560,128]{0,1:T(8,128)S(1)} %convolution_bitcast_fusion) | data formatting | bytes 2621440 | tf_op jit(solution)/shard_map/dot_general | solution.py:61
  21.2 1.5 %copy.36 = f32[2560,128]{1,0:T(8,128)} copy(f32[2560,128]{0,1:T(8,128)S(1)} %copy-done) | data formatting | bytes 2621440 | tf_op jit(solution)/shard_map/dot_general | solution.py:61
  22.7 1.7 %multiply_reduce_fusion = (f32[256,128]{1,0:T(8,128)S(1)}, f32[10,128]{1,0:T(8,128)S(1)}, f32[10,128]{1,0:T(8,128)S(1)}, f32[256,128]{1,0:T(8,128)S(1)}) fusion(f32[10,1,256,128]{3,2,0,1:T(8,128)S(1)} %bitcast.125, f32[10,128]{1,0:T(8,128)S(1)} %get-tuple-element.31, f32[256,128]{1,0:T(8,128)S(1)} %copy.37, f32[10,1,256,128]{3,2,0,1:T(8,128)} %bitcast.126, ...), kind=kLoop, calls=%fused_computation.2 | loop fusion | flops 2553344 | bytes 3035136 | tf_op jit(solution)/shard_map/reduce_sum | solution.py:69
  24.4 0.1 fusion.72
  24.6 13.2 %all-reduce = (f32[1,128]{1,0:T(1,128)S(1)}, f32[2304,2,1]{0,1,2:T(2,128)S(1)}, f32[2304,2,1]{0,1,2:T(2,128)S(1)}) all-reduce(f32[1,128]{1,0:T(1,128)S(1)} %add_bitcast_fusion, f32[2304,2,1]{0,1,2:T(2,128)S(1)} %reshape.498, f32[2304,2,1]{0,1,2:T(2,128)S(1)} %reshape.503), channel_id=1, replica_groups=mesh['groups'=2,'gx'=4,'gz'=2,'vert'=2] {'gz','vert'}, use_global_device_ids=true, to_apply=%region_2.0 | all-reduce | flops 9344 | bytes 74752 | tf_op jit(solution)/shard_map/psum | solution.py:81
  37.7 0.1 slice_bitcast_fusion.7
  37.8 0.6 pad_maximum_fusion
  38.4 4.9 %all-to-all-start = ((f32[4,576,2,1]{1,2,3,0:T(2,128)}), f32[4,576,2,1]{1,2,3,0:T(2,128)S(1)}, u32[]{:S(2)}, u32[]{:S(2)}) async-start(f32[4,576,2,1]{1,2,3,0:T(2,128)} %pad_maximum_fusion), calls=%async_computation | async-start | bytes 40960 | tf_op jit(solution)/shard_map/all_to_all | solution.py:88
  43.4 0.7 add.597
  44.0 0.1 reduce-scatter.3.cloned.1.call-update
  44.1 0.5 broadcast_multiply_fusion.2
  44.6 0.1 slice_bitcast_fusion.3
  44.7 0.6 pad_maximum_fusion.1
  45.3 3.7 %all-to-all-done = f32[4,576,2,1]{1,2,3,0:T(2,128)S(1)} async-done(((f32[4,576,2,1]{1,2,3,0:T(2,128)}), f32[4,576,2,1]{1,2,3,0:T(2,128)S(1)}, u32[]{:S(2)}, u32[]{:S(2)}) %all-to-all-start) | async-done | bytes 18464 | tf_op jit(solution)/shard_map/all_to_all | solution.py:88
  49.0 3.3 %all-to-all-start.1 = ((f32[4,576,2,1]{1,2,3,0:T(2,128)}), f32[4,576,2,1]{1,2,3,0:T(2,128)S(1)}, u32[]{:S(2)}, u32[]{:S(2)}) async-start(f32[4,576,2,1]{1,2,3,0:T(2,128)} %pad_maximum_fusion.1), calls=%async_computation.1 | async-start | bytes 40960 | tf_op jit(solution)/shard_map/all_to_all | solution.py:88
  52.2 0.3 fusion.64
  52.6 5.3 %all-to-all-done.1 = f32[4,576,2,1]{1,2,3,0:T(2,128)S(1)} async-done(((f32[4,576,2,1]{1,2,3,0:T(2,128)}), f32[4,576,2,1]{1,2,3,0:T(2,128)S(1)}, u32[]{:S(2)}, u32[]{:S(2)}) %all-to-all-start.1) | async-done | bytes 18464 | tf_op jit(solution)/shard_map/all_to_all | solution.py:88
  57.8 1.0 fusion.4
  58.8 1.3 %broadcast_multiply_fusion = f32[128,16]{0,1:T(8,128)} fusion(f32[128,16]{0,1:T(8,128)} %reduce-scatter.5.cloned.1.call-done), kind=kLoop, calls=%fused_computation.129 | loop fusion | flops 2048 | bytes 16384 | tf_op jit(solution)/shard_map/mul | solution.py:109
  60.1 43.6 %reduce-scatter.3.cloned.1.call-done = f32[16,128]{1,0:T(8,128)} async-done(((f32[256,128]{1,0:T(8,128)}), f32[16,128]{1,0:T(8,128)}) %reduce-scatter.3.cloned.1.call-update) | async-done | bytes 8208 | tf_op jit(solution)/shard_map/reduce_scatter | solution.py:97
  103.7 1.3 %broadcast_multiply_fusion.1 = f32[16,128]{1,0:T(8,128)} fusion(f32[16,128]{1,0:T(8,128)} %reduce-scatter.3.cloned.1.call-done), kind=kLoop, calls=%fused_computation.130 | loop fusion | flops 2048 | bytes 16384 | tf_op jit(solution)/shard_map/mul | solution.py:109
  (17 shorter events, 0.1 us)
Async XLA Ops:
  7.2 51.7 %reduce-scatter.5.cloned.1.call-start = ((), (), s32[]{:S(2)}) async-start(), calls=%async_computation.5 | async-start | bytes 73728 | tf_op jit(solution)/shard_map/reduce_scatter | solution.py:96
  15.8 1.8 %copy-start.2 = (f32[48,2560]{1,0:T(8,128)S(1)}, f32[48,2560]{1,0:T(8,128)}, u32[]{:S(2)}) copy-start(f32[48,2560]{1,0:T(8,128)} %fusion.70) | copy-start | bytes 1474564
  19.7 1.5 %copy-start = (f32[2560,128]{0,1:T(8,128)S(1)}, f32[2560,128]{0,1:T(8,128)}, u32[]{:S(2)}) copy-start(f32[2560,128]{0,1:T(8,128)} %convolution_bitcast_fusion.1) | copy-start | bytes 3932164
  21.2 1.5 %copy-start.1 = (f32[2560,128]{1,0:T(8,128)S(1)}, f32[2560,128]{1,0:T(8,128)}, u32[]{:S(2)}) copy-start(f32[2560,128]{1,0:T(8,128)} %copy.38) | copy-start | bytes 3932164
  38.4 10.6 %all-to-all-start = ((f32[4,576,2,1]{1,2,3,0:T(2,128)}), f32[4,576,2,1]{1,2,3,0:T(2,128)S(1)}, u32[]{:S(2)}, u32[]{:S(2)}) async-start(f32[4,576,2,1]{1,2,3,0:T(2,128)} %pad_maximum_fusion), calls=%async_computation | async-start | bytes 40960 | tf_op jit(solution)/shard_map/all_to_all | solution.py:88
  43.4 60.4 %reduce-scatter.3.cloned.1.call-start = ((), (), s32[]{:S(2)}) async-start(), calls=%async_computation.4 | async-start | bytes 139264 | tf_op jit(solution)/shard_map/reduce_scatter | solution.py:97
  49.0 8.9 %all-to-all-start.1 = ((f32[4,576,2,1]{1,2,3,0:T(2,128)}), f32[4,576,2,1]{1,2,3,0:T(2,128)S(1)}, u32[]{:S(2)}, u32[]{:S(2)}) async-start(f32[4,576,2,1]{1,2,3,0:T(2,128)} %pad_maximum_fusion.1), calls=%async_computation.1 | async-start | bytes 40960 | tf_op jit(solution)/shard_map/all_to_all | solution.py:88
Sparse Core Ops, SparseCore 0:
  13.2 32.7 reduce-scatter.4
  49.8 53.8 reduce-scatter.2
